TPU v7x, 256 devices: a whole 4x4x8 slice. The times are simulated.
256 devices in a mesh: wide: 32 (over z, x), narrow: 8 (over y, core).
Axes of the slice: x: 4, y: 4, z: 8, core: 2. Of those that a mesh axis runs over, the one named last changes fastest.
Arguments:
- hidden_in: bfloat16 [64, 8192], P(None, 'wide'), may hold values from -6 to 6
- attn_gain: bfloat16 [8192], P('wide'), may hold values from 0.099609375 to 1.8984375
- qkv_weight: bfloat16 [8192, 8, 10, 128], P('wide', 'narrow'), may hold values from -2 to 2
- qkv_bias: bfloat16 [8, 10, 128], P('narrow'), may hold values from -3 to 3
- cache_keys: bfloat16 [64, 8, 4096, 128], P('wide', 'narrow'), may hold values from -256 to 256
- cache_values: bfloat16 [64, 8, 4096, 128], P('wide', 'narrow'), may hold values from -10 to 10
- positions: int32 [64, 3, 4096], P('wide'), may hold values from 0 to 4095
- lengths: int32 [64], P('wide'), may hold values from 512 to 4095, as said below
- out_weight: bfloat16 [8192, 8192], P('narrow', 'wide'), may hold values from -0.0625 to 0.0625
- mlp_gain: bfloat16 [8192], P('wide'), may hold values from 0.099609375 to 1.8984375
- gate_up_weight: bfloat16 [8192, 2, 29568], P('wide', None, 'narrow'), may hold values from -0.0625 to 0.0625
- down_weight: bfloat16 [29568, 8192], P('narrow', 'wide'), may hold values from -0.03125 to 0.03125
Outputs:
- layer_out: bfloat16 [64, 8192], P(None, 'wide')
Inputs may be any that keep to these rules, and one draw needn't show every extreme that they name: Slots 0 to lengths[b] - 1 of request b are filled, the new token takes slot lengths[b], and some request has 4095.
All inputs are finite; a program needn't handle non-finite values.
Results may differ from a plain program's by a relative error of at most 0.01115.
The roundings to bfloat16 on the way count: a program that leaves them out, or rounds other values in their place, can miss the bound.
Values may be sent and summed in bfloat16 or wider, within the bound.
No kernel may reach another device: no remote copies, remote signals or barrier semaphores. Data moves between devices by JAX's collectives and lax.ppermute only.
A program may use at most 64 MiB of HBM per device.

v0:
```python
import math
import jax
import jax.numpy as jnp
from jax import lax
from jax.sharding import PartitionSpec as P

D = 8192
DH = 128
CACHE = 4096
norm_eps = 1e-06
rope_base = 1000000.0


def mrope_tables(position):
    half_width = DH // 2
    pair_index = jnp.arange(half_width)
    inv_freq = jnp.exp(pair_index.astype(jnp.float32) * (-2.0 * math.log(rope_base) / DH))
    component = (pair_index >= DH // 8).astype(jnp.int32) + (
        pair_index >= DH // 8 + 3 * DH // 16
    ).astype(jnp.int32)
    pos_float = position.astype(jnp.float32)
    chosen = jnp.where(
        component == 0,
        pos_float[..., 0, :, None],
        jnp.where(component == 1, pos_float[..., 1, :, None], pos_float[..., 2, :, None]),
    )
    angles = chosen * inv_freq
    return (jnp.cos(angles), jnp.sin(angles))


def rotate(values, cosine, sine_table):
    half_width = values.shape[-1] // 2
    leading = values[..., :half_width]
    trailing = values[..., half_width:]
    return jnp.concatenate(
        [leading * cosine - trailing * sine_table, trailing * cosine + leading * sine_table],
        axis=-1,
    )


def local(
    hidden_in,
    attn_gain,
    qkv_weight,
    qkv_bias,
    cache_keys,
    cache_values,
    positions,
    lengths,
    out_weight,
    mlp_gain,
    gate_up_weight,
    down_weight,
):
    score_scale = 1.0 / math.sqrt(DH)
    owned = lengths.shape[0]
    local_rows = hidden_in.shape[1]
    kv_local = qkv_weight.shape[1]
    slot_count = qkv_weight.shape[2]
    group_size = slot_count - 2
    width = kv_local * slot_count * DH
    inputs = hidden_in.astype(jnp.float32)
    local_squares = jnp.sum(inputs * inputs, axis=1)
    scaled = (inputs * attn_gain.astype(jnp.float32)).astype(jnp.bfloat16)
    weight_flat = qkv_weight.reshape(local_rows, width)
    inv_rms = 1.0 / jnp.sqrt(lax.psum(local_squares, "wide") / D + norm_eps)
    row_block = scaled
    factor = inv_rms
    projected = lax.psum_scatter(
        factor[:, None] * jnp.dot(row_block, weight_flat, preferred_element_type=jnp.float32),
        "wide",
        scatter_dimension=0,
        tiled=True,
    )
    projected = projected + qkv_bias.reshape(width).astype(jnp.float32)
    projected = projected.reshape(owned, kv_local, slot_count, DH)
    cosine, sine_table = mrope_tables(positions)
    keys_rot = rotate(cache_keys.astype(jnp.float32), cosine[:, None], sine_table[:, None]).astype(
        jnp.bfloat16
    )
    new_position = jnp.take_along_axis(positions, lengths[:, None, None], axis=2)
    cos_new, sin_new = mrope_tables(new_position)
    query = rotate(projected[:, :, :group_size], cos_new[:, None], sin_new[:, None]).astype(
        jnp.bfloat16
    )
    key_new = rotate(projected[:, :, group_size], cos_new, sin_new).astype(jnp.bfloat16)
    value_new = projected[:, :, group_size + 1].astype(jnp.bfloat16)
    scores = (
        jnp.einsum("rgjd,rgsd->rgjs", query, keys_rot, preferred_element_type=jnp.float32)
        * score_scale
    )
    own_score = (
        jnp.sum(query.astype(jnp.float32) * key_new.astype(jnp.float32)[:, :, None, :], axis=3)
        * score_scale
    )
    valid_slot = jnp.arange(CACHE)[None, None, None, :] < lengths[:, None, None, None]
    row_max = jnp.maximum(jnp.max(jnp.where(valid_slot, scores, -jnp.inf), axis=3), own_score)
    probabilities = jnp.where(valid_slot, jnp.exp(scores - row_max[..., None]), 0.0)
    own_prob = jnp.exp(own_score - row_max)
    totals = jnp.sum(probabilities, axis=3) + own_prob
    probs_rounded = probabilities.astype(jnp.bfloat16)
    own_rounded = own_prob.astype(jnp.bfloat16).astype(jnp.float32)
    weighted = jnp.einsum(
        "rgjs,rgsd->rgjd", probs_rounded, cache_values, preferred_element_type=jnp.float32
    )
    weighted = weighted + own_rounded[..., None] * value_new.astype(jnp.float32)[:, :, None, :]
    attended = (
        (weighted / totals[..., None])
        .astype(jnp.bfloat16)
        .reshape(owned, kv_local * group_size * DH)
    )
    head_partial = jnp.dot(
        lax.all_gather(attended, "wide", axis=0, tiled=True),
        out_weight,
        preferred_element_type=jnp.float32,
    )
    attn_out = lax.psum(head_partial, "narrow")
    residual = (inputs + attn_out).astype(jnp.bfloat16)
    resid_float = residual.astype(jnp.float32)
    resid_squares = jnp.sum(resid_float * resid_float, axis=1)
    scaled2 = (resid_float * mlp_gain.astype(jnp.float32)).astype(jnp.bfloat16)
    hidden_local = gate_up_weight.shape[2]
    gate_up_flat = gate_up_weight.reshape(local_rows, 2 * hidden_local)
    inv_rms2 = 1.0 / jnp.sqrt(lax.psum(resid_squares, "wide") / D + norm_eps)
    row_block = scaled2
    factor = inv_rms2
    gate_up = lax.psum_scatter(
        factor[:, None] * jnp.dot(row_block, gate_up_flat, preferred_element_type=jnp.float32),
        "wide",
        scatter_dimension=0,
        tiled=True,
    )
    hidden = (jax.nn.silu(gate_up[:, :hidden_local]) * gate_up[:, hidden_local:]).astype(
        jnp.bfloat16
    )
    down_partial = jnp.dot(
        lax.all_gather(hidden, "wide", axis=0, tiled=True),
        down_weight,
        preferred_element_type=jnp.float32,
    )
    mlp_out = lax.psum(down_partial, "narrow")
    return (resid_float + mlp_out).astype(jnp.bfloat16)


def solution(mesh):
    in_specs = (
        P(None, "wide"),
        P("wide"),
        P("wide", "narrow", None, None),
        P("narrow", None, None),
        P("wide", "narrow", None, None),
        P("wide", "narrow", None, None),
        P("wide", None, None),
        P("wide"),
        P("narrow", "wide"),
        P("wide"),
        P("wide", None, "narrow"),
        P("narrow", "wide"),
    )
    out_specs = P(None, "wide")
    return jax.shard_map(local, mesh=mesh, in_specs=in_specs, out_specs=out_specs, check_vma=False)
```

profile of v0, /device:TPU:2, one launch (start us, length us, event | category | flops | bytes accessed | tf_op | source)
XLA Modules:
  0.0 691.7 jit_solution(1203411043637431055)
XLA Ops:
  6.5 1.5 copy.20
  8.0 0.9 fusion.24
  8.9 73.7 %psum.28 = f32[64]{0:T(128)S(1)} all-reduce(f32[64]{0:T(128)S(1)} %fusion.24), channel_id=1, replica_groups=mesh['wide'=32,'narrow'=8] {'wide'}, use_global_device_ids=true, to_apply=%region_1.0 | all-reduce | flops 64 | bytes 512 | tf_op jit(solution)/shard_map/psum | solution.py:66
  83.3 1.8 convolution_multiply_fusion.2
  85.2 0.9 convert_element_type.179
  86.1 3.4 copy.22
  89.7 3.8 bitcast_convert_fusion
  93.8 1.4 gather_fusion
  95.6 19.8 %fusion.7 = (bf16[2,4096,64]{2,1,0:T(8,128)(2,1)}, bf16[2,4096,64]{2,1,0:T(8,128)(2,1)}) fusion(f32[2,1,4096,128]{3,2,0,1:T(8,128)} %bitcast_convert_fusion, f32[64]{0:T(128)S(1)} %multiply_exponential_fusion, f32[2,4096]{1,0:T(2,128)S(1)} %get-tuple-element.17, f32[2,4096]{1,0:T(2,128)S(1)} %get-tuple-element.18, f32[2,4096]{1,0:T(2,128)S(1)} %get-tuple-element.16, ...), kind=kLoop, calls=%fused_computation.15 | loop fusion | flops 5767168 | bytes 6390144 | tf_op jit(solution)/shard_map/concatenate | solution.py:35
  116.8 112.9 %all-reduce.11.cloned.1.call-done = f32[64,1280]{1,0:T(8,128)} async-done(((f32[64,1280]{1,0:T(8,128)}), f32[64,1280]{1,0:T(8,128)}) %all-reduce.11.cloned.1.call-update) | async-done | bytes 327696
  229.7 0.8 dynamic-slice_add_fusion
  231.0 3.6 select_reduce_fusion
  235.3 41.5 %all-gather = bf16[32,2,1024]{2,1,0:T(2,128)(2,1)S(1)} all-gather(bf16[1,2,1024]{2,1,0:T(2,128)(2,1)S(1)} %reshape.655), channel_id=1, replica_groups=mesh['wide'=32,'narrow'=8] {'wide'}, dimensions={0}, use_global_device_ids=true | all-gather | bytes 135168 | tf_op jit(solution)/shard_map/all_gather | solution.py:113
  276.9 0.8 fusion.52
  277.8 63.5 %all-reduce.7.cloned.1.call-done = f32[64,256]{1,0:T(8,128)} async-done(((f32[64,256]{1,0:T(8,128)}), f32[64,256]{1,0:T(8,128)}) %all-reduce.7.cloned.1.call-update) | async-done | bytes 65552 | tf_op jit(solution)/shard_map/psum | solution.py:117
  341.3 0.9 fusion.27
  342.3 71.1 %psum.30 = f32[64]{0:T(128)S(1)} all-reduce(f32[64]{0:T(128)S(1)} %get-tuple-element.8), channel_id=1, replica_groups=mesh['wide'=32,'narrow'=8] {'wide'}, use_global_device_ids=true, to_apply=%region_8.9 | all-reduce | flops 64 | bytes 512 | tf_op jit(solution)/shard_map/psum | solution.py:124
  413.4 4.6 convolution_multiply_fusion
  418.1 149.5 %all-reduce.13.cloned.1.call-done = f32[64,7392]{1,0:T(8,128)} async-done(((f32[64,7392]{1,0:T(8,128)}), f32[64,7392]{1,0:T(8,128)}) %all-reduce.13.cloned.1.call-update) | async-done | bytes 1892368
  567.6 1.1 fusion.36
  568.7 48.7 %all-gather.1 = bf16[32,2,3696]{2,1,0:T(2,128)(2,1)S(1)} all-gather(bf16[1,2,3696]{2,1,0:T(2,128)(2,1)S(1)} %fusion.36), channel_id=1, replica_groups=mesh['wide'=32,'narrow'=8] {'wide'}, dimensions={0}, use_global_device_ids=true | all-gather | bytes 487872 | tf_op jit(solution)/shard_map/all_gather | solution.py:137
  617.7 2.6 fusion.53
  620.3 63.4 %all-reduce.9.cloned.1.call-done = f32[64,256]{1,0:T(8,128)} async-done(((f32[64,256]{1,0:T(8,128)}), f32[64,256]{1,0:T(8,128)}) %all-reduce.9.cloned.1.call-update) | async-done | bytes 65552 | tf_op jit(solution)/shard_map/psum | solution.py:141
  683.7 1.5 fusion.29
  (57 shorter events, 4.0 us)
Async XLA Ops:
  6.5 228.3 %copy-start = (bf16[2,1,4096,128]{3,2,1,0:T(8,128)(2,1)S(1)}, bf16[2,1,4096,128]{3,2,1,0:T(8,128)(2,1)}, u32[]{:S(2)}) copy-start(bf16[2,1,4096,128]{3,2,1,0:T(8,128)(2,1)} %param.17) | copy-start | bytes 6291460
  6.5 83.0 %copy-start.4 = (s32[2]{0:T(128)S(1)}, s32[2]{0:T(128)}, u32[]{:S(2)}) copy-start(s32[2]{0:T(128)} %param.19) | copy-start | bytes 28
  6.5 223.2 %all-reduce.11.cloned.1.call-start = ((), (), s32[]{:S(2)}) async-start(), calls=%async_computation.2 | async-start | bytes 655360
  85.1 256.2 %all-reduce.7.cloned.1.call-start = ((), (), s32[]{:S(2)}) async-start(), calls=%async_computation | async-start | bytes 131072 | tf_op jit(solution)/shard_map/psum | solution.py:117
  95.6 20.0 %copy-start.6 = (u32[256]{0:T(256)S(1)}, u32[256]{0:T(256)}, u32[]{:S(2)}) copy-start(u32[256]{0:T(256)} %constant.61) | copy-start | bytes 3076
  95.6 21.2 %copy-start.3 = (bf16[1,10,128]{2,1,0:T(8,128)(2,1)S(1)}, bf16[1,10,128]{2,1,0:T(8,128)(2,1)}, u32[]{:S(2)}) copy-start(bf16[1,10,128]{2,1,0:T(8,128)(2,1)} %param.15) | copy-start | bytes 7684
  231.0 45.9 %copy-start.1 = (bf16[1024,256]{1,0:T(8,128)(2,1)S(1)}, bf16[1024,256]{1,0:T(8,128)(2,1)}, u32[]{:S(2)}) copy-start(bf16[1024,256]{1,0:T(8,128)(2,1)} %param.20) | copy-start | bytes 1572868
  231.0 46.8 %copy-start.5 = (bf16[256]{0:T(256)(128)(2,1)S(1)}, bf16[256]{0:T(256)(128)(2,1)}, u32[]{:S(2)}) copy-start(bf16[256]{0:T(256)(128)(2,1)} %param.21) | copy-start | bytes 1540
  231.0 110.4 %copy-start.2 = (bf16[64,256]{1,0:T(8,128)(2,1)S(1)}, bf16[64,256]{1,0:T(8,128)(2,1)}, u32[]{:S(2)}) copy-start(bf16[64,256]{1,0:T(8,128)(2,1)} %param.12) | copy-start | bytes 98308
  277.7 289.9 %all-reduce.13.cloned.1.call-start = ((), (), s32[]{:S(2)}) async-start(), calls=%async_computation.3 | async-start | bytes 3801088
  418.0 265.6 %all-reduce.9.cloned.1.call-start = ((), (), s32[]{:S(2)}) async-start(), calls=%async_computation.1 | async-start | bytes 131072 | tf_op jit(solution)/shard_map/psum | solution.py:141
Sparse Core Ops, SparseCore 0:
  85.3 144.4 all-reduce.10
  277.9 63.4 all-reduce.6
  418.2 149.3 all-reduce.12
  620.4 63.1 all-reduce.8
where the time goes:
time: 692 us
  waiting for transfers between devices  389 us (56%)
  blocking collectives  235 us (34%)
  other arithmetic  31.6 us (5%)
  between operations  14 us (2%)
  matrix products  13.9 us (2%)
  local copies, waits for them, and re-layouts  7.72 us (1%)
    unnamed x6, waiting for transfers between devices  262 us
    psum x1, blocking collectives, local(): inv_rms = 1.0 / jnp.sqrt(lax.psum(local_squares, 'wide') / D + norm_eps)  73.7 us
    psum x1, blocking collectives, local(): inv_rms2 = 1.0 / jnp.sqrt(lax.psum(resid_squares, 'wide') / D + norm_eps)  71.1 us
    psum x1, waiting for transfers between devices, local(): attn_out = lax.psum(head_partial, 'narrow')  63.5 us
    psum x1, waiting for transfers between devices, local(): mlp_out = lax.psum(down_partial, 'narrow')  63.4 us
    all_gather x1, blocking collectives, local(): lax.all_gather(hidden, 'wide', axis=0, tiled=True)  48.7 us
    all_gather x1, blocking collectives, local(): lax.all_gather(attended, 'wide', axis=0, tiled=True)  41.5 us
    concatenate x2, other arithmetic, rotate(): jnp.concatenate([leading * cosine - trailing * sine_table, trailing * cos...  19.8 us
  transfers between devices with their start and end apart: 4, of which 4 were waited for; matrix products, arithmetic and copies ran while one was open for 4% of the time, Pallas kernels for 0%

commit v1 on v0

--- a/solution.py
+++ b/solution.py
@@ -134,7 +134,9 @@
         jnp.bfloat16
     )
     down_partial = jnp.dot(
-        lax.all_gather(hidden, "wide", axis=0, tiled=True),
+        jnp.concatenate(
+            lax.all_to_all(jnp.stack([hidden] * lax.axis_size("wide")), "wide", 0, 0), axis=0
+        ),
         down_weight,
         preferred_element_type=jnp.float32,
     )

time: 692 us -> 662 us (0.957)
  blocking collectives: 235 us -> 206 us
    all_gather x1 -> x0, blocking collectives: 48.7 us -> none  [local(): lax.all_gather(hidden, 'wide', axis=0, tiled=True)]
    all_to_all x0 -> x1, blocking collectives: none -> 19.5 us  [local(): lax.all_to_all(jnp.stack([hidden] * lax.axis_size('wide')), 'wide', 0, 0)]
  transfers between devices with their start and end apart: 4 -> 4, of which waited for: 4 -> 4; matrix products, arithmetic and copies ran while one was open for 4% -> 5% of each run, Pallas kernels for 0% -> 0%
where the time goes in v1:
time: 662 us; the launch traced here: 661 us
  waiting for transfers between devices  388 us (59%)
  blocking collectives  206 us (31%)
  other arithmetic  31.6 us (5%)
  between operations  14 us (2%)
  matrix products  13.9 us (2%)
  local copies, waits for them, and re-layouts  7.97 us (1%)
    unnamed x6, waiting for transfers between devices  262 us
    psum x1, blocking collectives, local(): inv_rms = 1.0 / jnp.sqrt(lax.psum(local_squares, 'wide') / D + norm_eps)  73.7 us
    psum x1, blocking collectives, local(): inv_rms2 = 1.0 / jnp.sqrt(lax.psum(resid_squares, 'wide') / D + norm_eps)  71.1 us
    psum x1, waiting for transfers between devices, local(): attn_out = lax.psum(head_partial, 'narrow')  63.5 us
    psum x1, waiting for transfers between devices, local(): mlp_out = lax.psum(down_partial, 'narrow')  61.7 us
    all_gather x1, blocking collectives, local(): lax.all_gather(attended, 'wide', axis=0, tiled=True)  41.5 us
    concatenate x2, other arithmetic, rotate(): jnp.concatenate([leading * cosine - trailing * sine_table, trailing * cos...  19.8 us
    all_to_all x1, blocking collectives, local(): lax.all_to_all(jnp.stack([hidden] * lax.axis_size('wide')), 'wide', 0, 0)  19.5 us
  transfers between devices with their start and end apart: 4, of which 4 were waited for; matrix products, arithmetic and copies ran while one was open for 5% of the time, Pallas kernels for 0%

profile of v1, /device:TPU:2, one launch (start us, length us, event | category | flops | bytes accessed | tf_op | source)
XLA Modules:
  0.0 661.1 jit_solution(6523068267170204250)
XLA Ops:
  6.5 1.5 copy.20
  8.0 0.9 fusion.24
  8.9 73.7 %psum.28 = f32[64]{0:T(128)S(1)} all-reduce(f32[64]{0:T(128)S(1)} %fusion.24), channel_id=1, replica_groups=mesh['wide'=32,'narrow'=8] {'wide'}, use_global_device_ids=true, to_apply=%region_1.0 | all-reduce | flops 64 | bytes 512 | tf_op jit(solution)/shard_map/psum | solution.py:66
  83.3 1.8 convolution_multiply_fusion.2
  85.2 0.9 convert_element_type.179
  86.1 3.4 copy.22
  89.7 3.8 bitcast_convert_fusion
  93.8 1.4 gather_fusion
  95.6 19.8 %fusion.7 = (bf16[2,4096,64]{2,1,0:T(8,128)(2,1)}, bf16[2,4096,64]{2,1,0:T(8,128)(2,1)}) fusion(f32[2,1,4096,128]{3,2,0,1:T(8,128)} %bitcast_convert_fusion, f32[64]{0:T(128)S(1)} %multiply_exponential_fusion, f32[2,4096]{1,0:T(2,128)S(1)} %get-tuple-element.17, f32[2,4096]{1,0:T(2,128)S(1)} %get-tuple-element.18, f32[2,4096]{1,0:T(2,128)S(1)} %get-tuple-element.16, ...), kind=kLoop, calls=%fused_computation.15 | loop fusion | flops 5767168 | bytes 6390144 | tf_op jit(solution)/shard_map/concatenate | solution.py:35
  116.8 112.9 %all-reduce.11.cloned.1.call-done = f32[64,1280]{1,0:T(8,128)} async-done(((f32[64,1280]{1,0:T(8,128)}), f32[64,1280]{1,0:T(8,128)}) %all-reduce.11.cloned.1.call-update) | async-done | bytes 327696
  229.7 0.8 dynamic-slice_add_fusion
  231.0 3.6 select_reduce_fusion
  235.3 41.5 %all-gather = bf16[32,2,1024]{2,1,0:T(2,128)(2,1)S(1)} all-gather(bf16[1,2,1024]{2,1,0:T(2,128)(2,1)S(1)} %reshape.661), channel_id=1, replica_groups=mesh['wide'=32,'narrow'=8] {'wide'}, dimensions={0}, use_global_device_ids=true | all-gather | bytes 135168 | tf_op jit(solution)/shard_map/all_gather | solution.py:113
  276.9 0.8 fusion.51
  277.8 63.5 %all-reduce.7.cloned.1.call-done = f32[64,256]{1,0:T(8,128)} async-done(((f32[64,256]{1,0:T(8,128)}), f32[64,256]{1,0:T(8,128)}) %all-reduce.7.cloned.1.call-update) | async-done | bytes 65552 | tf_op jit(solution)/shard_map/psum | solution.py:117
  341.3 0.9 fusion.27
  342.3 71.1 %psum.30 = f32[64]{0:T(128)S(1)} all-reduce(f32[64]{0:T(128)S(1)} %get-tuple-element.8), channel_id=1, replica_groups=mesh['wide'=32,'narrow'=8] {'wide'}, use_global_device_ids=true, to_apply=%region_8.9 | all-reduce | flops 64 | bytes 512 | tf_op jit(solution)/shard_map/psum | solution.py:124
  413.4 4.6 convolution_multiply_fusion
  418.1 149.5 %all-reduce.13.cloned.1.call-done = f32[64,7392]{1,0:T(8,128)} async-done(((f32[64,7392]{1,0:T(8,128)}), f32[64,7392]{1,0:T(8,128)}) %all-reduce.13.cloned.1.call-update) | async-done | bytes 1892368
  567.6 1.1 fusion.35
  568.9 19.5 %all_to_all.5 = bf16[32,2,3696]{2,1,0:T(2,128)(2,1)S(1)} all-to-all(bf16[32,2,3696]{2,1,0:T(2,128)(2,1)S(1)} %stack.2), channel_id=1, replica_groups=mesh['wide'=32,'narrow'=8] {'wide'}, dimensions={0} | all-to-all | bytes 946176 | tf_op jit(solution)/shard_map/all_to_all | solution.py:138
  588.8 2.6 fusion.52
  591.4 61.7 %all-reduce.9.cloned.1.call-done = f32[64,256]{1,0:T(8,128)} async-done(((f32[64,256]{1,0:T(8,128)}), f32[64,256]{1,0:T(8,128)}) %all-reduce.9.cloned.1.call-update) | async-done | bytes 65552 | tf_op jit(solution)/shard_map/psum | solution.py:143
  653.1 1.5 fusion.29
  (58 shorter events, 4.2 us)
Async XLA Ops:
  6.5 228.3 %copy-start = (bf16[2,1,4096,128]{3,2,1,0:T(8,128)(2,1)S(1)}, bf16[2,1,4096,128]{3,2,1,0:T(8,128)(2,1)}, u32[]{:S(2)}) copy-start(bf16[2,1,4096,128]{3,2,1,0:T(8,128)(2,1)} %param.17) | copy-start | bytes 6291460
  6.5 83.0 %copy-start.4 = (s32[2]{0:T(128)S(1)}, s32[2]{0:T(128)}, u32[]{:S(2)}) copy-start(s32[2]{0:T(128)} %param.19) | copy-start | bytes 28
  6.5 223.2 %all-reduce.11.cloned.1.call-start = ((), (), s32[]{:S(2)}) async-start(), calls=%async_computation.3 | async-start | bytes 655360
  85.1 256.2 %all-reduce.7.cloned.1.call-start = ((), (), s32[]{:S(2)}) async-start(), calls=%async_computation.1 | async-start | bytes 131072 | tf_op jit(solution)/shard_map/psum | solution.py:117
  95.6 20.0 %copy-start.6 = (u32[256]{0:T(256)S(1)}, u32[256]{0:T(256)}, u32[]{:S(2)}) copy-start(u32[256]{0:T(256)} %constant.61) | copy-start | bytes 3076
  95.6 21.2 %copy-start.3 = (bf16[1,10,128]{2,1,0:T(8,128)(2,1)S(1)}, bf16[1,10,128]{2,1,0:T(8,128)(2,1)}, u32[]{:S(2)}) copy-start(bf16[1,10,128]{2,1,0:T(8,128)(2,1)} %param.15) | copy-start | bytes 7684
  231.0 45.9 %copy-start.1 = (bf16[1024,256]{1,0:T(8,128)(2,1)S(1)}, bf16[1024,256]{1,0:T(8,128)(2,1)}, u32[]{:S(2)}) copy-start(bf16[1024,256]{1,0:T(8,128)(2,1)} %param.20) | copy-start | bytes 1572868
  231.0 46.8 %copy-start.5 = (bf16[256]{0:T(256)(128)(2,1)S(1)}, bf16[256]{0:T(256)(128)(2,1)}, u32[]{:S(2)}) copy-start(bf16[256]{0:T(256)(128)(2,1)} %param.21) | copy-start | bytes 1540
  231.0 110.4 %copy-start.2 = (bf16[64,256]{1,0:T(8,128)(2,1)S(1)}, bf16[64,256]{1,0:T(8,128)(2,1)}, u32[]{:S(2)}) copy-start(bf16[64,256]{1,0:T(8,128)(2,1)} %param.12) | copy-start | bytes 98308
  277.7 289.9 %all-reduce.13.cloned.1.call-start = ((), (), s32[]{:S(2)}) async-start(), calls=%async_computation.4 | async-start | bytes 3801088
  418.0 235.1 %all-reduce.9.cloned.1.call-start = ((), (), s32[]{:S(2)}) async-start(), calls=%async_computation.2 | async-start | bytes 131072 | tf_op jit(solution)/shard_map/psum | solution.py:143
Sparse Core Ops, SparseCore 0:
  85.3 144.4 all-reduce.10
  277.9 63.4 all-reduce.6
  418.2 149.3 all-reduce.12
  591.5 61.5 all-reduce.8
